TPU v7x, 512 devices: a whole 4x4x16 slice. The times are simulated.
512 devices in a mesh: dp: 16 (over y, z_lo), page: 32 (over z_hi, x, core).
Axes of the slice: x: 4, y: 4, z: 16 (z_hi: 4, z_lo: 4; z = z_hi * 4 + z_lo), core: 2. Of those that a mesh axis runs over, the one named last changes fastest.
Arguments:
- queries: bfloat16 [16, 32, 128, 1024], P('dp', 'page'), may hold values from -200 to 200
- keys: bfloat16 [16, 32, 128, 1024], P('dp', 'page'), may hold values from -6 to 6
- values: bfloat16 [16, 32, 128, 1024], P('dp', 'page'), may hold values from -6 to 6
- grad_out: bfloat16 [16, 32, 128, 1024], P('dp', 'page'), may hold values from -6 to 6
- out_weight: bfloat16 [1024, 1024], P(('dp', 'page')), may hold values from -0.1875 to 0.1875
- partners: int32 [16, 2, 32], P('dp'), may hold values from 0 to 31, as said below
- block_mask: int32 [16, 32, 2, 1, 1], P('dp', 'page'), may hold values 0 or 1
- buckets: int32 [16, 32, 3, 1, 1], P('dp', 'page'), may hold values from 0 to 31
- bias_table: float32 [32, 16], replicated, may hold values from -4 to 4
Outputs:
- layer_out: bfloat16 [16, 32, 128, 1024], P('dp', 'page')
- query_grad: bfloat16 [16, 32, 128, 1024], P('dp', 'page')
- key_grad: bfloat16 [16, 32, 128, 1024], P('dp', 'page')
- value_grad: bfloat16 [16, 32, 128, 1024], P('dp', 'page')
- weight_grad: float32 [1024, 1024], P(('dp', 'page'))
Inputs may be any that keep to these rules, and one draw needn't show every extreme that they name: partners[f, r, partners[f, r, p]] = p and partners[f, r, p] != p.
All inputs are finite; a program needn't handle non-finite values. No bound on the sum of `block_mask` on one device may be relied on, other than what follows from the above.
Results may differ from a plain program's by a relative error of at most 0.025.
Values may be sent and summed in bfloat16 or wider, within the bound.
No kernel may reach another device: no remote copies, remote signals or barrier semaphores. Data moves between devices by JAX's collectives and lax.ppermute only.
A program may use at most 64 MiB of HBM per device.

v0:
```python
import math

import jax
import jax.numpy as jnp
from jax import lax
from jax.sharding import PartitionSpec as P

H = 16
BLOCK = 128
ROUNDS = 2


heads_per_step = 4
neg_large = -1e30


def head_steps(query_rows, key_set, value_set, grad_rows, bias_blocks, allowed):
    page_len, width = query_rows.shape
    key_count = key_set.shape[0]
    groups = key_count // page_len
    head_dim = width // H
    step_count = H // heads_per_step
    block_count = page_len // BLOCK
    scale = 1.0 / math.sqrt(head_dim)

    def split(array):
        return array.reshape(array.shape[0], step_count, heads_per_step, head_dim).transpose(
            1, 0, 2, 3
        )

    bias_split = bias_blocks.reshape(
        groups, block_count, block_count, step_count, heads_per_step
    ).transpose(3, 4, 1, 0, 2)
    allow_wide = allowed.transpose(1, 0, 2)[None, :, None, :, :, None]

    def one_step(inputs):
        q_part, k_part, v_part, g_part, b_part = inputs
        scores = (
            jnp.einsum("qhd,khd->hqk", q_part, k_part, preferred_element_type=jnp.float32) * scale
        )
        scores = scores.reshape(heads_per_step, block_count, BLOCK, groups, block_count, BLOCK)
        scores = scores + b_part[:, :, None, :, :, None]
        scores = jnp.where(allow_wide, scores, neg_large).reshape(
            heads_per_step, page_len, key_count
        )
        top = jnp.max(scores, axis=-1, keepdims=True)
        expo = jnp.exp(scores - top)
        prob = expo / jnp.sum(expo, axis=-1, keepdims=True)
        prob_b = prob.astype(jnp.bfloat16)
        attn_part = jnp.einsum(
            "hqk,khd->qhd", prob_b, v_part, preferred_element_type=jnp.float32
        ).astype(jnp.bfloat16)
        dprob = jnp.einsum("qhd,khd->hqk", g_part, v_part, preferred_element_type=jnp.float32)
        row_dot = jnp.sum(g_part.astype(jnp.float32) * attn_part.astype(jnp.float32), axis=-1).T[
            :, :, None
        ]
        dscore = (prob * (dprob - row_dot) * scale).astype(jnp.bfloat16)
        q_grad = jnp.einsum("hqk,khd->qhd", dscore, k_part, preferred_element_type=jnp.float32)
        k_grad = jnp.einsum("hqk,qhd->khd", dscore, q_part, preferred_element_type=jnp.float32)
        v_grad = jnp.einsum("hqk,qhd->khd", prob_b, g_part, preferred_element_type=jnp.float32)
        return (attn_part, q_grad, k_grad, v_grad)

    results = lax.map(
        one_step,
        (split(query_rows), split(key_set), split(value_set), split(grad_rows), bias_split),
    )

    def join(array):
        return array.transpose(1, 0, 2, 3).reshape(array.shape[1], width)

    return (join(results[0]), join(results[1]), join(results[2]), join(results[3]))


def shards(queries, keys, values, grad_out, out_weight, partners, block_mask, buckets, bias_table):
    weight = lax.all_gather(out_weight, ("dp", "page"), axis=0, tiled=True)
    q_page = queries[0, 0]
    k_page = keys[0, 0]
    v_page = values[0, 0]
    g_page = grad_out[0, 0]
    page_len, width = q_page.shape
    block_count = page_len // BLOCK
    peers = lax.axis_size("page")
    piece_rows = page_len // peers
    mates = partners[0]
    kv_pair = jnp.stack([k_page, v_page])
    d_attn = lax.dot_general(
        g_page, weight, (((1,), (1,)), ((), ())), preferred_element_type=jnp.float32
    ).astype(jnp.bfloat16)

    def spread(stacked):
        pieces = stacked.reshape(2, peers, piece_rows, width)
        return lax.all_to_all(pieces, "page", split_axis=1, concat_axis=1, tiled=True)

    def collect(received, chosen):
        picked = jnp.take(received, chosen, axis=1)
        back = lax.all_to_all(picked, "page", split_axis=2, concat_axis=2, tiled=True)
        return back.reshape(2, chosen.shape[0], page_len, width)

    fetched = jnp.concatenate(
        [collect(spread(kv_pair), mates[r : r + 1]) for r in range(ROUNDS)], 1
    )
    key_set = jnp.concatenate([k_page[None], fetched[0]], 0).reshape(-1, width)
    value_set = jnp.concatenate([v_page[None], fetched[1]], 0).reshape(-1, width)
    bucket_ids = buckets[0, 0]
    one_hot = bucket_ids[..., None] == jnp.arange(bias_table.shape[0], dtype=jnp.int32)
    bias_blocks = jnp.sum(jnp.where(one_hot[..., None], bias_table, 0.0), axis=-2)
    allowed = jnp.concatenate(
        [jnp.ones((1, block_count, block_count), bool), block_mask[0, 0] == 1], 0
    )
    attn, q_grad, k_grad, v_grad = head_steps(
        q_page, key_set, value_set, d_attn, bias_blocks, allowed
    )
    layer_out = jnp.dot(attn, weight, preferred_element_type=jnp.float32).astype(jnp.bfloat16)
    weight_grad = lax.psum_scatter(
        lax.dot_general(attn, g_page, (((0,), (0,)), ((), ())), preferred_element_type=jnp.float32),
        ("dp", "page"),
        scatter_dimension=0,
        tiled=True,
    )
    outgoing = (
        jnp.stack([k_grad[page_len:], v_grad[page_len:]])
        .reshape(2, ROUNDS, page_len, width)
        .astype(jnp.bfloat16)
    )

    def give_back(terms, chosen):
        round_count = terms.shape[1]
        pieces = terms.reshape(2, round_count, peers, piece_rows, width)
        received = lax.all_to_all(pieces, "page", split_axis=2, concat_axis=2, tiled=True)
        picked = jnp.stack([jnp.take(received[:, 0], chosen[0], axis=1)], 1)
        back = lax.all_to_all(picked, "page", split_axis=2, concat_axis=2, tiled=True)
        return back.reshape(2, round_count, page_len, width)

    returned = jnp.concatenate(
        [give_back(outgoing[:, r : r + 1], mates[r : r + 1]) for r in range(ROUNDS)], 1
    )
    totals = jnp.stack([k_grad[:page_len], v_grad[:page_len]]) + jnp.sum(
        returned.astype(jnp.float32), axis=1
    )
    key_grad = totals[0].astype(jnp.bfloat16)[None, None]
    value_grad = totals[1].astype(jnp.bfloat16)[None, None]
    return (
        layer_out[None, None],
        q_grad.astype(jnp.bfloat16)[None, None],
        key_grad,
        value_grad,
        weight_grad,
    )


def solution(mesh):
    in_specs = (
        P("dp", "page", None, None),
        P("dp", "page", None, None),
        P("dp", "page", None, None),
        P("dp", "page", None, None),
        P(("dp", "page"), None),
        P("dp", None, None),
        P("dp", "page", None, None, None),
        P("dp", "page", None, None, None),
        P(),
    )
    out_specs = (
        P("dp", "page", None, None),
        P("dp", "page", None, None),
        P("dp", "page", None, None),
        P("dp", "page", None, None),
        P(("dp", "page"), None),
    )
    return jax.shard_map(shards, mesh=mesh, in_specs=in_specs, out_specs=out_specs, check_vma=False)
```

profile of v0, /device:TPU:6, one launch (start us, length us, event | category | flops | bytes accessed | tf_op | source)
XLA Modules:
  0.0 1547.1 jit_solution(18248375689373877247)
XLA Ops:
  10.5 18.2 %all-to-all-start = ((bf16[2,32,4,1024]{3,2,0,1:T(4,128)(2,1)}), bf16[2,32,4,1024]{3,2,0,1:T(4,128)(2,1)S(1)}, u32[]{:S(2)}, u32[]{:S(2)}) async-start(bf16[2,32,4,1024]{3,2,0,1:T(4,128)(2,1)} %pad_maximum_fusion.4), calls=%async_computation | async-start | bytes 1048576 | tf_op jit(solution)/shard_map/all_to_all | solution.py:92
  28.7 27.3 %all-to-all-done = bf16[2,32,4,1024]{3,2,0,1:T(4,128)(2,1)S(1)} async-done(((bf16[2,32,4,1024]{3,2,0,1:T(4,128)(2,1)}), bf16[2,32,4,1024]{3,2,0,1:T(4,128)(2,1)S(1)}, u32[]{:S(2)}, u32[]{:S(2)}) %all-to-all-start) | async-done | bytes 524320 | tf_op jit(solution)/shard_map/all_to_all | solution.py:92
  58.3 11.4 all-to-all-start.1
  72.6 24.7 %all-to-all-done.1 = bf16[2,1,32,4,1024]{4,3,0,1,2:T(4,128)(2,1)S(1)} async-done(((bf16[2,1,32,4,1024]{4,3,0,1,2:T(4,128)(2,1)}), bf16[2,1,32,4,1024]{4,3,0,1,2:T(4,128)(2,1)S(1)}, u32[]{:S(2)}, u32[]{:S(2)}) %all-to-all-start.1) | async-done | bytes 524320 | tf_op jit(solution)/shard_map/all_to_all | solution.py:96
  97.4 11.5 all-to-all-start.2
  111.1 25.6 %all-to-all-done.2 = bf16[2,1,32,4,1024]{4,3,0,1,2:T(4,128)(2,1)S(1)} async-done(((bf16[2,1,32,4,1024]{4,3,0,1,2:T(4,128)(2,1)}), bf16[2,1,32,4,1024]{4,3,0,1,2:T(4,128)(2,1)S(1)}, u32[]{:S(2)}, u32[]{:S(2)}) %all-to-all-start.2) | async-done | bytes 524320 | tf_op jit(solution)/shard_map/all_to_all | solution.py:96
  144.0 710.9 %all-gather.3.cloned.1.call-done = bf16[512,2,1024]{2,1,0:T(2,128)(2,1)} async-done(((bf16[1,2,1024]{2,1,0:T(2,128)(2,1)}), bf16[512,2,1024]{2,1,0:T(2,128)(2,1)}) %all-gather.3.cloned.1.call-update) | async-done | bytes 2097168 | tf_op jit(solution)/shard_map/all_gather | solution.py:75
  854.9 2.7 reshape.233
  859.3 50.1 %while.16 = (s32[]{:T(128)}, bf16[4,128,4,64]{1,3,2,0:T(8,128)(2,1)}, bf16[4,128,4,64]{1,3,2,0:T(8,128)(2,1)}, f32[4,384,4,64]{1,3,2,0:T(8,128)}, f32[4,384,4,64...) while((s32[]{:T(128)}, ...), condition=%wide.region_5.7_spmd, body=%wide.region_1.6_spmd.sunk | while | flops 205817472 | bytes 5562152 | solution.py:63
  860.1 2.1 fusion.126
  862.2 2.2 bitcast_dynamic-update-slice_fusion.2
  868.7 2.2 fusion.130
  872.6 2.1 fusion.126
  874.8 2.2 bitcast_dynamic-update-slice_fusion.2
  881.3 2.3 fusion.130
  885.2 2.1 fusion.126
  887.3 2.2 bitcast_dynamic-update-slice_fusion.2
  893.8 2.2 fusion.130
  899.8 2.2 bitcast_dynamic-update-slice_fusion.2
  906.3 2.2 fusion.130
  911.7 2.7 copy.125
  918.5 3.8 copy.126
  922.3 3.9 fusion.69
  927.3 10.1 all-to-all-start.3
  938.4 31.1 %all-to-all-done.3 = bf16[2,1,32,4,1024]{4,3,0,1,2:T(4,128)(2,1)S(1)} async-done(((bf16[2,1,32,4,1024]{4,3,0,1,2:T(4,128)(2,1)}), bf16[2,1,32,4,1024]{4,3,0,1,2:T(4,128)(2,1)S(1)}, u32[]{:S(2)}, u32[]{:S(2)}) %all-to-all-start.3) | async-done | bytes 524320 | tf_op jit(solution)/shard_map/all_to_all | solution.py:129
  969.5 6.6 all-to-all-start.5
  980.3 27.9 %all-to-all-done.5 = bf16[2,1,32,4,1024]{4,3,0,1,2:T(4,128)(2,1)S(1)} async-done(((bf16[2,1,32,4,1024]{4,3,0,1,2:T(4,128)(2,1)}), bf16[2,1,32,4,1024]{4,3,0,1,2:T(4,128)(2,1)S(1)}, u32[]{:S(2)}, u32[]{:S(2)}) %all-to-all-start.5) | async-done | bytes 524320 | tf_op jit(solution)/shard_map/all_to_all | solution.py:129
  1008.2 7.0 all-to-all-start.4
  1015.4 3.6 fusion.72
  1023.2 19.7 %all-to-all-done.4 = bf16[2,1,32,4,1024]{4,3,0,1,2:T(4,128)(2,1)S(1)} async-done(((bf16[2,1,32,4,1024]{4,3,0,1,2:T(4,128)(2,1)}), bf16[2,1,32,4,1024]{4,3,0,1,2:T(4,128)(2,1)S(1)}, u32[]{:S(2)}, u32[]{:S(2)}) %all-to-all-start.4) | async-done | bytes 524320 | tf_op jit(solution)/shard_map/all_to_all | solution.py:131
  1042.9 11.7 all-to-all-start.6
  1063.3 467.6 %all-reduce.3.cloned.1.call-done = f32[1024,1024]{1,0:T(8,128)} async-done(((f32[1024,1024]{1,0:T(8,128)}), f32[1024,1024]{1,0:T(8,128)}) %all-reduce.3.cloned.1.call-update) | async-done | bytes 4194320
  (139 shorter events, 80.5 us)
Async XLA Ops:
  7.2 850.5 %copy-start = (bf16[1,1,128,1024]{3,2,1,0:T(8,128)(2,1)S(1)}, bf16[1,1,128,1024]{3,2,1,0:T(8,128)(2,1)}, u32[]{:S(2)}) copy-start(bf16[1,1,128,1024]{3,2,1,0:T(8,128)(2,1)} %param.18) | copy-start | bytes 786436
  7.2 21.5 %copy-start.6 = (s32[1,2,32]{2,1,0:T(2,128)S(1)}, s32[1,2,32]{2,1,0:T(2,128)}, u32[]{:S(2)}) copy-start(s32[1,2,32]{2,1,0:T(2,128)} %param.20) | copy-start | bytes 772
  10.5 45.5 %all-to-all-start = ((bf16[2,32,4,1024]{3,2,0,1:T(4,128)(2,1)}), bf16[2,32,4,1024]{3,2,0,1:T(4,128)(2,1)S(1)}, u32[]{:S(2)}, u32[]{:S(2)}) async-start(bf16[2,32,4,1024]{3,2,0,1:T(4,128)(2,1)} %pad_maximum_fusion.4), calls=%async_computation | async-start | bytes 1048576 | tf_op jit(solution)/shard_map/all_to_all | solution.py:92
  58.3 39.0 %all-to-all-start.1 = ((bf16[2,1,32,4,1024]{4,3,0,1,2:T(4,128)(2,1)}), bf16[2,1,32,4,1024]{4,3,0,1,2:T(4,128)(2,1)S(1)}, u32[]{:S(2)}, u32[]{:S(2)}) async-start(bf16[2,1,32,4,1024]{4,3,0,1,2:T(4,128)(2,1)} %fusion.71), calls=%async_computation.1 | async-start | bytes 1048576 | tf_op jit(solution)/shard_map/all_to_all | solution.py:96
  69.7 785.2 %all-gather.3.cloned.1.call-start = ((), (), s32[]{:S(2)}) async-start(), calls=%async_computation.7 | async-start | bytes 2101248 | tf_op jit(solution)/shard_map/all_gather | solution.py:75
  70.5 38.5 %copy-start.5 = (bf16[1,1,128,1024]{3,2,1,0:T(8,128)(2,1)S(1)}, bf16[1,1,128,1024]{3,2,1,0:T(8,128)(2,1)}, u32[]{:S(2)}) copy-start(bf16[1,1,128,1024]{3,2,1,0:T(8,128)(2,1)} %param.15) | copy-start | bytes 786436
  71.5 38.3 %copy-start.9 = (s32[1,1,3,1,1]{2,4,3,1,0:T(1,128)S(1)}, s32[1,1,3,1,1]{2,4,3,1,0:T(1,128)}, u32[]{:S(2)}) copy-start(s32[1,1,3,1,1]{2,4,3,1,0:T(1,128)} %param.22) | copy-start | bytes 40
  71.5 38.4 %copy-start.8 = (f32[32,16]{0,1:T(8,128)S(1)}, f32[32,16]{0,1:T(8,128)}, u32[]{:S(2)}) copy-start(f32[32,16]{0,1:T(8,128)} %param.23) | copy-start | bytes 6148
  71.5 38.5 %copy-start.10 = (s32[1,1,2,1,1]{2,4,3,1,0:T(1,128)S(1)}, s32[1,1,2,1,1]{2,4,3,1,0:T(1,128)}, u32[]{:S(2)}) copy-start(s32[1,1,2,1,1]{2,4,3,1,0:T(1,128)} %param.21) | copy-start | bytes 28
  97.4 39.4 %all-to-all-start.2 = ((bf16[2,1,32,4,1024]{4,3,0,1,2:T(4,128)(2,1)}), bf16[2,1,32,4,1024]{4,3,0,1,2:T(4,128)(2,1)S(1)}, u32[]{:S(2)}, u32[]{:S(2)}) async-start(bf16[2,1,32,4,1024]{4,3,0,1,2:T(4,128)(2,1)} %fusion.70), calls=%async_computation.2 | async-start | bytes 1048576 | tf_op jit(solution)/shard_map/all_to_all | solution.py:96
  139.1 1.0 copy-start.3
  140.8 1.7 copy-start.4
  860.1 4.3 copy-start.11
  862.2 2.2 copy-start.12
  872.6 4.3 copy-start.11
  874.8 2.2 copy-start.12
  885.2 4.3 copy-start.11
  887.3 2.2 copy-start.12
  897.7 4.3 copy-start.11
  899.8 2.2 copy-start.12
  926.2 11.1 copy-start.2
  927.3 48.8 %copy-start.7 = (s32[1,2,32]{2,1,0:T(2,128)S(1)}, s32[1,2,32]{2,1,0:T(2,128)}, u32[]{:S(2)}) copy-start(s32[1,2,32]{2,1,0:T(2,128)} %param.20) | copy-start | bytes 772
  927.3 42.2 %all-to-all-start.3 = ((bf16[2,1,32,4,1024]{4,3,0,1,2:T(4,128)(2,1)}), bf16[2,1,32,4,1024]{4,3,0,1,2:T(4,128)(2,1)S(1)}, u32[]{:S(2)}, u32[]{:S(2)}) async-start(bf16[2,1,32,4,1024]{4,3,0,1,2:T(4,128)(2,1)} %copy.127), calls=%async_computation.3 | async-start | bytes 1048576 | tf_op jit(solution)/shard_map/all_to_all | solution.py:129
  969.5 38.7 %all-to-all-start.5 = ((bf16[2,1,32,4,1024]{4,3,0,1,2:T(4,128)(2,1)}), bf16[2,1,32,4,1024]{4,3,0,1,2:T(4,128)(2,1)S(1)}, u32[]{:S(2)}, u32[]{:S(2)}) async-start(bf16[2,1,32,4,1024]{4,3,0,1,2:T(4,128)(2,1)} %copy.131), calls=%async_computation.5 | async-start | bytes 1048576 | tf_op jit(solution)/shard_map/all_to_all | solution.py:129
  1008.2 34.7 %all-to-all-start.4 = ((bf16[2,1,32,4,1024]{4,3,0,1,2:T(4,128)(2,1)}), bf16[2,1,32,4,1024]{4,3,0,1,2:T(4,128)(2,1)S(1)}, u32[]{:S(2)}, u32[]{:S(2)}) async-start(bf16[2,1,32,4,1024]{4,3,0,1,2:T(4,128)(2,1)} %select_bitcast_fusion.1), calls=%async_computation.4 | async-start | bytes 1048576 | tf_op jit(solution)/shard_map/all_to_all | solution.py:131
  1015.1 515.7 %all-reduce.3.cloned.1.call-start = ((), (), s32[]{:S(2)}) async-start(), calls=%async_computation.8 | async-start | bytes 8388608
  1042.8 14.8 copy-start.1
  1042.9 490.9 %all-to-all-start.6 = ((bf16[2,1,32,4,1024]{4,3,0,1,2:T(4,128)(2,1)}), bf16[2,1,32,4,1024]{4,3,0,1,2:T(4,128)(2,1)}, u32[]{:S(2)}, u32[]{:S(2)}) async-start(bf16[2,1,32,4,1024]{4,3,0,1,2:T(4,128)(2,1)} %select_bitcast_fusion), calls=%async_computation.6 | async-start | bytes 1048576 | tf_op jit(solution)/shard_map/all_to_all | solution.py:131
Sparse Core Ops, SparseCore 0:
  72.7 782.1 all-gather.2
  1021.4 509.3 all-reduce.2
where the time goes:
time: 1550 us
  waiting for transfers between devices  1340 us (86%)
  starting transfers between devices  76.8 us (5%)
  local copies, waits for them, and re-layouts  51.9 us (3%)
  matrix products  50.2 us (3%)
  other arithmetic  18.3 us (1%)
    all_gather x1, waiting for transfers between devices, shards(): weight = lax.all_gather(out_weight, ('dp', 'page'), axis=0, tiled=True)  711 us
    unnamed x3, waiting for transfers between devices  468 us
    all_to_all x2, waiting for transfers between devices, give_back(): lax.all_to_all(pieces, 'page', split_axis=2, concat_axis=2, tiled=True)  58.9 us
    all_to_all x2, waiting for transfers between devices, collect(): lax.all_to_all(picked, 'page', split_axis=2, concat_axis=2, tiled=True)  50.3 us
  transfers between devices with their start and end apart: 9, of which 8 were waited for; matrix products, arithmetic and copies ran while one was open for 2% of the time, Pallas kernels for 0%

commit v1 on v0

--- a/solution.py
+++ b/solution.py
@@ -72,7 +72,9 @@
 
 
 def shards(queries, keys, values, grad_out, out_weight, partners, block_mask, buckets, bias_table):
-    weight = lax.all_gather(out_weight, ("dp", "page"), axis=0, tiled=True)
+    weight = lax.all_gather(
+        lax.all_gather(out_weight, "page", axis=0, tiled=True), "dp", axis=0, tiled=True
+    )
     q_page = queries[0, 0]
     k_page = keys[0, 0]
     v_page = values[0, 0]
@@ -96,9 +98,7 @@
         back = lax.all_to_all(picked, "page", split_axis=2, concat_axis=2, tiled=True)
         return back.reshape(2, chosen.shape[0], page_len, width)
 
-    fetched = jnp.concatenate(
-        [collect(spread(kv_pair), mates[r : r + 1]) for r in range(ROUNDS)], 1
-    )
+    fetched = collect(spread(kv_pair), mates)
     key_set = jnp.concatenate([k_page[None], fetched[0]], 0).reshape(-1, width)
     value_set = jnp.concatenate([v_page[None], fetched[1]], 0).reshape(-1, width)
     bucket_ids = buckets[0, 0]
@@ -111,12 +111,16 @@
         q_page, key_set, value_set, d_attn, bias_blocks, allowed
     )
     layer_out = jnp.dot(attn, weight, preferred_element_type=jnp.float32).astype(jnp.bfloat16)
-    weight_grad = lax.psum_scatter(
-        lax.dot_general(attn, g_page, (((0,), (0,)), ((), ())), preferred_element_type=jnp.float32),
-        ("dp", "page"),
-        scatter_dimension=0,
-        tiled=True,
+    partial = lax.dot_general(
+        attn, g_page, (((0,), (0,)), ((), ())), preferred_element_type=jnp.float32
     )
+    dp_size = lax.axis_size("dp")
+    rows_each = width // (dp_size * peers)
+    partial = partial.reshape(dp_size, peers, rows_each, width)
+    partial = lax.psum_scatter(partial, "dp", scatter_dimension=0, tiled=True)
+    partial = partial.reshape(1, peers, rows_each * width // 128, 128)
+    partial = lax.psum_scatter(partial, "page", scatter_dimension=1, tiled=True)
+    weight_grad = partial.reshape(rows_each, width)
     outgoing = (
         jnp.stack([k_grad[page_len:], v_grad[page_len:]])
         .reshape(2, ROUNDS, page_len, width)
@@ -127,13 +131,13 @@
         round_count = terms.shape[1]
         pieces = terms.reshape(2, round_count, peers, piece_rows, width)
         received = lax.all_to_all(pieces, "page", split_axis=2, concat_axis=2, tiled=True)
-        picked = jnp.stack([jnp.take(received[:, 0], chosen[0], axis=1)], 1)
+        picked = jnp.stack(
+            [jnp.take(received[:, r], chosen[r], axis=1) for r in range(round_count)], 1
+        )
         back = lax.all_to_all(picked, "page", split_axis=2, concat_axis=2, tiled=True)
         return back.reshape(2, round_count, page_len, width)
 
-    returned = jnp.concatenate(
-        [give_back(outgoing[:, r : r + 1], mates[r : r + 1]) for r in range(ROUNDS)], 1
-    )
+    returned = give_back(outgoing, mates)
     totals = jnp.stack([k_grad[:page_len], v_grad[:page_len]]) + jnp.sum(
         returned.astype(jnp.float32), axis=1
     )

time: 1550 us -> 589 us (0.38)
  waiting for transfers between devices: 1340 us -> 362 us
  blocking collectives: 0 us -> 62.9 us
  starting transfers between devices: 76.8 us -> 59.9 us
    all_gather x1, waiting for transfers between devices: 711 us -> 103 us  [shards(): lax.all_gather(lax.all_gather(out_weight, 'page', axis=0, tiled=True), 'd...]
    unnamed x3, waiting for transfers between devices: 468 us -> 0.05 us
    reduce_scatter x0 -> x2, waiting for transfers between devices: none -> 148 us  [the longest x1 107 us: shards(): partial = lax.psum_scatter(partial, 'page', scatter_dimension=1, tiled=True)]
    all_gather x0 -> x1, blocking collectives: none -> 62.9 us  [shards(): lax.all_gather(out_weight, 'page', axis=0, tiled=True)]
    all_to_all x2 -> x1, waiting for transfers between devices: 50.3 us -> 0.01 us  [collect(): lax.all_to_all(picked, 'page', split_axis=2, concat_axis=2, tiled=True)]
    all_to_all x2 -> x1, waiting for transfers between devices: 19.7 us -> 49 us  [give_back(): lax.all_to_all(picked, 'page', split_axis=2, concat_axis=2, tiled=True)]
    all_to_all x1, waiting for transfers between devices: 27.3 us -> 0.01 us  [spread(): lax.all_to_all(pieces, 'page', split_axis=1, concat_axis=1, tiled=True)]
    all_to_all x2 -> x1, waiting for transfers between devices: 58.9 us -> 62.7 us  [give_back(): lax.all_to_all(pieces, 'page', split_axis=2, concat_axis=2, tiled=True)]
  transfers between devices with their start and end apart: 9 -> 7, of which waited for: 8 -> 5; matrix products, arithmetic and copies ran while one was open for 2% -> 5% of each run, Pallas kernels for 0% -> 0%
where the time goes in v1:
time: 589 us; the launch traced here: 586 us
  waiting for transfers between devices  362 us (61%)
  blocking collectives  62.9 us (11%)
  starting transfers between devices  59.9 us (10%)
  local copies, waits for them, and re-layouts  41.2 us (7%)
  matrix products  38.2 us (6%)
  between operations  14.3 us (2%)
  other arithmetic  6.82 us (1%)
    reduce_scatter x1, waiting for transfers between devices, shards(): partial = lax.psum_scatter(partial, 'page', scatter_dimension=1, tiled=True)  107 us
    all_gather x1, waiting for transfers between devices, shards(): lax.all_gather(lax.all_gather(out_weight, 'page', axis=0, tiled=True), 'd...  103 us
    all_gather x1, blocking collectives, shards(): lax.all_gather(out_weight, 'page', axis=0, tiled=True)  62.9 us
    all_to_all x1, waiting for transfers between devices, give_back(): lax.all_to_all(pieces, 'page', split_axis=2, concat_axis=2, tiled=True)  62.7 us
    all_to_all x1, waiting for transfers between devices, give_back(): lax.all_to_all(picked, 'page', split_axis=2, concat_axis=2, tiled=True)  49 us
    reduce_scatter x1, waiting for transfers between devices, shards(): partial = lax.psum_scatter(partial, 'dp', scatter_dimension=0, tiled=True)  40.6 us
    all_to_all x1, starting transfers between devices, spread(): lax.all_to_all(pieces, 'page', split_axis=1, concat_axis=1, tiled=True)  18.2 us
    all_to_all x1, starting transfers between devices, collect(): lax.all_to_all(picked, 'page', split_axis=2, concat_axis=2, tiled=True)  16 us
  transfers between devices with their start and end apart: 7, of which 5 were waited for; matrix products, arithmetic and copies ran while one was open for 5% of the time, Pallas kernels for 0%

profile of v1, /device:TPU:6, one launch (start us, length us, event | category | flops | bytes accessed | tf_op | source)
XLA Modules:
  0.0 585.8 jit_solution(6858723879362208658)
XLA Ops:
  10.5 18.2 %all-to-all-start = ((bf16[2,32,4,1024]{3,2,0,1:T(4,128)(2,1)}), bf16[2,32,4,1024]{3,2,0,1:T(4,128)(2,1)S(1)}, u32[]{:S(2)}, u32[]{:S(2)}) async-start(bf16[2,32,4,1024]{3,2,0,1:T(4,128)(2,1)} %pad_maximum_fusion.4), calls=%async_computation | async-start | bytes 1048576 | tf_op jit(solution)/shard_map/all_to_all | solution.py:94
  28.8 62.9 %all-gather = bf16[32,2,1024]{2,1,0:T(2,128)(2,1)S(1)} all-gather(bf16[1,2,1024]{2,1,0:T(2,128)(2,1)S(1)} %bitcast.250), channel_id=1, replica_groups=mesh['dp'=16,'page'=32] {'page'}, dimensions={0}, use_global_device_ids=true | all-gather | bytes 135168 | tf_op jit(solution)/shard_map/all_gather | solution.py:76
  94.9 2.1 copy.138
  97.0 16.0 %all-to-all-start.1 = ((bf16[2,2,32,4,1024]{4,1,3,0,2:T(2,128)(2,1)}), bf16[2,2,32,4,1024]{4,1,3,0,2:T(2,128)(2,1)S(1)}, u32[]{:S(2)}, u32[]{:S(2)}) async-start(bf16[2,2,32,4,1024]{4,1,3,0,2:T(2,128)(2,1)} %copy.138), calls=%async_computation.1 | async-start | bytes 2097152 | tf_op jit(solution)/shard_map/all_to_all | solution.py:98
  115.1 102.7 %all-gather.3.cloned.1.call-done = bf16[1024,1024]{1,0:T(8,128)(2,1)} async-done(((bf16[64,1024]{1,0:T(8,128)(2,1)}), bf16[1024,1024]{1,0:T(8,128)(2,1)}) %all-gather.3.cloned.1.call-update) | async-done | bytes 2097168 | tf_op jit(solution)/shard_map/all_gather | solution.py:75
  217.8 2.4 convolution_convert_fusion.2
  221.1 1.6 fusion.83
  223.9 1.5 copy.140
  225.4 1.4 reshape_reshape.6
  228.0 1.5 copy.143
  230.2 31.8 %while.16 = (s32[]{:T(128)}, bf16[4,128,4,64]{1,3,2,0:T(8,128)(2,1)S(1)}, bf16[4,128,4,64]{1,3,2,0:T(8,128)(2,1)}, f32[4,384,4,64]{1,3,2,0:T(8,128)}, f32[4,384,...) while((s32[]{:T(128)}, ...), condition=%wide.region_5.6_spmd, body=%wide.region_1.0_spmd.sunk | while | flops 205817472 | bytes 5552368 | solution.py:63
  231.7 1.5 bitcast_dynamic-update-slice_fusion.2
  233.3 1.6 fusion.123
  239.7 1.5 bitcast_dynamic-update-slice_fusion.2
  241.3 1.6 fusion.123
  247.6 1.5 bitcast_dynamic-update-slice_fusion.2
  249.2 1.6 fusion.123
  255.6 1.5 bitcast_dynamic-update-slice_fusion.2
  257.2 1.6 fusion.123
  268.9 1.6 copy.148
  270.5 14.1 %all-to-all-start.2 = ((bf16[2,2,32,4,1024]{4,3,0,1,2:T(4,128)(2,1)}), bf16[2,2,32,4,1024]{4,3,0,1,2:T(4,128)(2,1)S(1)}, u32[]{:S(2)}, u32[]{:S(2)}) async-start(bf16[2,2,32,4,1024]{4,3,0,1,2:T(4,128)(2,1)} %copy.148), calls=%async_computation.2 | async-start | bytes 2097152 | tf_op jit(solution)/shard_map/all_to_all | solution.py:133
  284.6 2.7 fusion.69
  287.4 62.7 %all-to-all-done.2 = bf16[2,2,32,4,1024]{4,3,0,1,2:T(4,128)(2,1)S(1)} async-done(((bf16[2,2,32,4,1024]{4,3,0,1,2:T(4,128)(2,1)}), bf16[2,2,32,4,1024]{4,3,0,1,2:T(4,128)(2,1)S(1)}, u32[]{:S(2)}, u32[]{:S(2)}) %all-to-all-start.2) | async-done | bytes 1048608 | tf_op jit(solution)/shard_map/all_to_all | solution.py:133
  354.3 1.4 copy.151
  355.8 11.5 %all-to-all-start.3 = ((bf16[2,2,32,4,1024]{4,3,0,1,2:T(4,128)(2,1)}), bf16[2,2,32,4,1024]{4,3,0,1,2:T(4,128)(2,1)S(1)}, u32[]{:S(2)}, u32[]{:S(2)}) async-start(bf16[2,2,32,4,1024]{4,3,0,1,2:T(4,128)(2,1)} %copy.151), calls=%async_computation.3 | async-start | bytes 2097152 | tf_op jit(solution)/shard_map/all_to_all | solution.py:137
  367.3 1.9 slice.68
  369.2 1.9 slice.69
  371.1 1.8 copy.158
  372.9 2.1 fusion.67
  375.0 49.0 %all-to-all-done.3 = bf16[2,2,32,4,1024]{4,3,0,1,2:T(4,128)(2,1)S(1)} async-done(((bf16[2,2,32,4,1024]{4,3,0,1,2:T(4,128)(2,1)}), bf16[2,2,32,4,1024]{4,3,0,1,2:T(4,128)(2,1)S(1)}, u32[]{:S(2)}, u32[]{:S(2)}) %all-to-all-start.3) | async-done | bytes 1048608 | tf_op jit(solution)/shard_map/all_to_all | solution.py:137
  426.0 40.6 %reduce-scatter.3.cloned.1.call-done = f32[1,32,2,1024]{3,1,2,0:T(8,128)} async-done(((f32[16,32,2,1024]{3,1,2,0:T(8,128)}), f32[1,32,2,1024]{3,1,2,0:T(8,128)}) %reduce-scatter.3.cloned.1.call-update) | async-done | bytes 262160 | tf_op jit(solution)/shard_map/reduce_scatter | solution.py:120
  470.6 107.3 %reduce-scatter.5.cloned.1.call-done = f32[1,1,16,128]{3,2,1,0:T(8,128)} async-done(((f32[1,32,16,128]{3,2,1,0:T(8,128)}), f32[1,1,16,128]{3,2,1,0:T(8,128)}) %reduce-scatter.5.cloned.1.call-update) | async-done | bytes 8208 | tf_op jit(solution)/shard_map/reduce_scatter | solution.py:122
  (132 shorter events, 50.1 us)
Async XLA Ops:
  7.2 210.6 %copy-start = (bf16[1,1,128,1024]{3,2,1,0:T(8,128)(2,1)S(1)}, bf16[1,1,128,1024]{3,2,1,0:T(8,128)(2,1)}, u32[]{:S(2)}) copy-start(bf16[1,1,128,1024]{3,2,1,0:T(8,128)(2,1)} %param.16) | copy-start | bytes 786436
  7.2 21.6 %copy-start.13 = (bf16[2,1024]{1,0:T(2,128)(2,1)S(1)}, bf16[2,1024]{1,0:T(2,128)(2,1)}, u32[]{:S(2)}) copy-start(bf16[2,1024]{1,0:T(2,128)(2,1)} %param.17) | copy-start | bytes 12292
  7.2 85.2 %copy-start.14 = (s32[1,2,32]{2,1,0:T(2,128)S(1)}, s32[1,2,32]{2,1,0:T(2,128)}, u32[]{:S(2)}) copy-start(s32[1,2,32]{2,1,0:T(2,128)} %param.18) | copy-start | bytes 772
  10.5 82.0 %all-to-all-start = ((bf16[2,32,4,1024]{3,2,0,1:T(4,128)(2,1)}), bf16[2,32,4,1024]{3,2,0,1:T(4,128)(2,1)S(1)}, u32[]{:S(2)}, u32[]{:S(2)}) async-start(bf16[2,32,4,1024]{3,2,0,1:T(4,128)(2,1)} %pad_maximum_fusion.4), calls=%async_computation | async-start | bytes 1048576 | tf_op jit(solution)/shard_map/all_to_all | solution.py:94
  28.7 189.1 %all-gather.3.cloned.1.call-start = ((), (), s32[]{:S(2)}) async-start(), calls=%async_computation.6 | async-start | bytes 2228224 | tf_op jit(solution)/shard_map/all_gather | solution.py:75
  94.9 18.2 %copy-start.9 = (bf16[1,1,128,1024]{3,2,1,0:T(8,128)(2,1)S(1)}, bf16[1,1,128,1024]{3,2,1,0:T(8,128)(2,1)}, u32[]{:S(2)}) copy-start(bf16[1,1,128,1024]{3,2,1,0:T(8,128)(2,1)} %param.15) | copy-start | bytes 786436
  94.9 18.6 %copy-start.10 = (bf16[1,1,128,1024]{3,2,1,0:T(8,128)(2,1)S(1)}, bf16[1,1,128,1024]{3,2,1,0:T(8,128)(2,1)}, u32[]{:S(2)}) copy-start(bf16[1,1,128,1024]{3,2,1,0:T(8,128)(2,1)} %param.14) | copy-start | bytes 786436
  97.0 16.9 %copy-start.11 = (bf16[1,1,128,1024]{3,2,1,0:T(8,128)(2,1)S(1)}, bf16[1,1,128,1024]{3,2,1,0:T(8,128)(2,1)}, u32[]{:S(2)}) copy-start(bf16[1,1,128,1024]{3,2,1,0:T(8,128)(2,1)} %param.13) | copy-start | bytes 786436
  97.0 17.8 %copy-start.15 = (s32[1,1,3,1,1]{2,4,3,1,0:T(1,128)S(1)}, s32[1,1,3,1,1]{2,4,3,1,0:T(1,128)}, u32[]{:S(2)}) copy-start(s32[1,1,3,1,1]{2,4,3,1,0:T(1,128)} %param.20) | copy-start | bytes 40
  97.0 17.8 %copy-start.12 = (f32[32,16]{0,1:T(8,128)S(1)}, f32[32,16]{0,1:T(8,128)}, u32[]{:S(2)}) copy-start(f32[32,16]{0,1:T(8,128)} %param.21) | copy-start | bytes 6148
  97.0 18.0 %copy-start.16 = (s32[1,1,2,1,1]{2,4,3,1,0:T(1,128)S(1)}, s32[1,1,2,1,1]{2,4,3,1,0:T(1,128)}, u32[]{:S(2)}) copy-start(s32[1,1,2,1,1]{2,4,3,1,0:T(1,128)} %param.19) | copy-start | bytes 28
  97.0 124.1 %all-to-all-start.1 = ((bf16[2,2,32,4,1024]{4,1,3,0,2:T(2,128)(2,1)}), bf16[2,2,32,4,1024]{4,1,3,0,2:T(2,128)(2,1)S(1)}, u32[]{:S(2)}, u32[]{:S(2)}) async-start(bf16[2,2,32,4,1024]{4,1,3,0,2:T(2,128)(2,1)} %copy.138), calls=%async_computation.1 | async-start | bytes 2097152 | tf_op jit(solution)/shard_map/all_to_all | solution.py:98
  223.9 3.0 copy-start.4
  227.9 2.2 copy-start.5
  227.9 2.2 copy-start.6
  227.9 2.2 copy-start.7
  262.0 22.6 %copy-start.8 = (bf16[4,128,4,64]{1,3,2,0:T(8,128)(2,1)}, bf16[4,128,4,64]{1,3,2,0:T(8,128)(2,1)S(1)}, u32[]{:S(2)}) copy-start(bf16[4,128,4,64]{1,3,2,0:T(8,128)(2,1)S(1)} %get-tuple-element.66) | copy-start | bytes 786436
  270.5 79.6 %all-to-all-start.2 = ((bf16[2,2,32,4,1024]{4,3,0,1,2:T(4,128)(2,1)}), bf16[2,2,32,4,1024]{4,3,0,1,2:T(4,128)(2,1)S(1)}, u32[]{:S(2)}, u32[]{:S(2)}) async-start(bf16[2,2,32,4,1024]{4,3,0,1,2:T(4,128)(2,1)} %copy.148), calls=%async_computation.2 | async-start | bytes 2097152 | tf_op jit(solution)/shard_map/all_to_all | solution.py:133
  284.6 182.1 %reduce-scatter.3.cloned.1.call-start = ((), (), s32[]{:S(2)}) async-start(), calls=%async_computation.7 | async-start | bytes 4456448 | tf_op jit(solution)/shard_map/reduce_scatter | solution.py:120
  355.8 17.1 %copy-start.1 = (bf16[1024,1024]{1,0:T(8,128)(2,1)S(1)}, bf16[1024,1024]{1,0:T(8,128)(2,1)}, u32[]{:S(2)}) copy-start(bf16[1024,1024]{1,0:T(8,128)(2,1)} %all-gather.3.cloned.1.call-done) | copy-start | bytes 6291460
  355.8 68.3 %all-to-all-start.3 = ((bf16[2,2,32,4,1024]{4,3,0,1,2:T(4,128)(2,1)}), bf16[2,2,32,4,1024]{4,3,0,1,2:T(4,128)(2,1)S(1)}, u32[]{:S(2)}, u32[]{:S(2)}) async-start(bf16[2,2,32,4,1024]{4,3,0,1,2:T(4,128)(2,1)} %copy.151), calls=%async_computation.3 | async-start | bytes 2097152 | tf_op jit(solution)/shard_map/all_to_all | solution.py:137
  367.3 210.7 %reduce-scatter.5.cloned.1.call-start = ((), (), s32[]{:S(2)}) async-start(), calls=%async_computation.8 | async-start | bytes 270336 | tf_op jit(solution)/shard_map/reduce_scatter | solution.py:122
  425.5 43.3 %copy-start.2 = (f32[128,4,4,64]{0,3,2,1:T(8,128)S(1)}, f32[128,4,4,64]{0,3,2,1:T(8,128)}, u32[]{:S(2)}) copy-start(f32[128,4,4,64]{0,3,2,1:T(8,128)} %slice.68) | copy-start | bytes 1572868
  425.5 43.3 %copy-start.3 = (f32[128,4,4,64]{0,3,2,1:T(8,128)S(1)}, f32[128,4,4,64]{0,3,2,1:T(8,128)}, u32[]{:S(2)}) copy-start(f32[128,4,4,64]{0,3,2,1:T(8,128)} %slice.69) | copy-start | bytes 1572868
Sparse Core Ops, SparseCore 0:
  92.5 125.2 all-gather.2
  288.2 178.3 reduce-scatter.2
  471.0 106.9 reduce-scatter.4
